TPU v7x, 512 devices: a whole 4x8x8 slice. The times are simulated.
512 devices in a mesh: sub: 128 (over z_hi, x, y, core), scen: 4 (over z_lo).
Axes of the slice: x: 4, y: 8, z: 8 (z_hi: 2, z_lo: 4; z = z_hi * 4 + z_lo), core: 2. Of those that a mesh axis runs over, the one named last changes fastest.
Arguments:
- inverse_matrix: bfloat16 [128, 1024, 1024], P('sub'), may hold values from -1 to 1
- objective_grad: bfloat16 [48, 128, 64, 1024], P(None, 'sub', 'scen'), may hold values from -6 to 6
- final_adjoint: float32 [128, 64, 1024], P('sub', 'scen'), may hold values from -6 to 6
- companion: float32 [128, 1024], P('sub'), may hold values from 0.95 to 0.995
- port_node: int32 [128, 4, 8], P('sub'), may hold values from 0 to 1023
- line_count: int32 [128, 4], P('sub'), may hold values from 1 to 8, as said below
- line_delay: int32 [128, 4, 8], P('sub'), may hold values from 24 to 47, as said below
- line_admittance: float32 [128, 4, 8], P('sub'), may hold values from 0.3 to 1.2
- later_history: float32 [128, 4, 8, 48, 64], P('sub', None, None, None, 'scen'), may hold values from -6 to 6
- conv_node: int32 [128, 16], P('sub'), may hold values from 0 to 1023
- conv_drive: float32 [128, 48, 64, 16], P('sub', None, 'scen'), may hold values from -0.25 to 0.25
- fault_bus: int32 [64], P('scen'), may hold values from 0 to 131071
- fault_current: float32 [48, 64], P(None, 'scen'), may hold values from -12 to 12
- fault_voltage: float32 [48, 64], P(None, 'scen'), may hold values from -2 to 2
Outputs:
- adjoint_start: float32 [128, 64, 1024], P('sub', 'scen')
- earlier_history: float32 [128, 4, 8, 48, 64], P('sub', None, None, None, 'scen')
- control_sens: float32 [128, 16], P('sub')
- fault_sens: float32 [64], P('scen')
Inputs may be any that keep to these rules, and one draw needn't show every extreme that they name: line_count[p, e] equals line_count of the partner subnetwork in the opposite direction; the most is reached in every draw. `line_delay`: both ends of a line have the same delay; both ends of the range are reached in every draw.
All inputs are finite; a program needn't handle non-finite values.
Results may differ from a plain program's by a relative error of at most 0.0088.
Values sent between devices are 32-bit elements; how exact they have to be, the bound alone decides.
No kernel may reach another device: no remote copies, remote signals or barrier semaphores. Data moves between devices by JAX's collectives and lax.ppermute only.
A program may use at most 64 MiB of HBM per device.

v0:
```python
import jax
import jax.numpy as jnp
from jax import lax
from jax.sharding import PartitionSpec as P

PRECISE = lax.Precision.HIGHEST


def passed_along(value, axis, steps):
    count = lax.axis_size(axis)
    pairs = [(source, (source + steps) % count) for source in range(count)]
    return lax.ppermute(value, axis, pairs)


def body(
    inverse_matrix,
    objective_grad,
    final_adjoint,
    companion,
    port_node,
    line_count,
    line_delay,
    line_admittance,
    later_history,
    conv_node,
    conv_drive,
    fault_bus,
    fault_current,
    fault_voltage,
):
    node_count = inverse_matrix.shape[1]
    scen_rows = objective_grad.shape[2]
    slot_count = port_node.shape[2]
    port_total = 4 * slot_count
    conv_count = conv_node.shape[1]
    block_len = later_history.shape[3] // 2
    blocks = objective_grad.shape[0] // block_len
    sub_count = lax.axis_size("sub")
    grid_width = max(2, sub_count // 16)
    offsets = (1, -1, grid_width, -grid_width)
    opposite = (1, 0, 3, 2)
    sub_index = lax.axis_index("sub")
    weights = inverse_matrix[0]
    live_mask = (lax.iota(jnp.int32, slot_count)[None, :] < line_count[0][:, None]).astype(
        jnp.float32
    )
    node_iota = lax.iota(jnp.int32, node_count)
    pick_table = jnp.concatenate(
        [
            node_iota[:, None] == port_node[0].reshape(port_total)[None, :],
            node_iota[:, None] == conv_node[0][None, :],
        ],
        axis=1,
    ).astype(jnp.float32)
    spread_table = jnp.transpose(pick_table[:, :port_total])
    line_scale = (line_admittance[0] * live_mask).reshape(port_total)
    fault_table = (node_iota[None, :] == (fault_bus - sub_index * node_count)[:, None]).astype(
        jnp.float32
    )
    window = later_history[0]
    adjoint_next = final_adjoint[0]
    control_local = jnp.zeros((conv_count,), jnp.float32)
    fault_local = jnp.zeros((scen_rows,), jnp.float32)
    block_rows = lax.iota(jnp.int32, block_len)
    time_iota = lax.iota(jnp.int32, 2 * block_len)

    def one_step(adjoint_prev, inputs):
        grad_now, inflow_now, current_now = inputs
        right_side = (
            grad_now.astype(jnp.float32)
            + companion[0][None, :] * adjoint_prev
            + inflow_now
            + current_now[:, None] * fault_table
        )
        adjoint = jnp.dot(
            right_side.astype(jnp.bfloat16), weights, preferred_element_type=jnp.float32
        )
        return (adjoint, adjoint)

    for block_id in reversed(range(blocks)):
        block_start = block_id * block_len
        target = block_rows[None, None, :] + line_delay[0][:, :, None] - block_len
        time_table = (target[..., None] == time_iota).astype(jnp.float32)
        picked = (
            jnp.einsum("ecji,ecis->jsec", time_table, window, precision=PRECISE).reshape(
                block_len * scen_rows, port_total
            )
            * line_scale[None, :]
        )
        inflow = jnp.dot(picked, spread_table, precision=PRECISE).reshape(
            block_len, scen_rows, node_count
        )
        adjoint_next, adjoint_block = lax.scan(
            one_step,
            adjoint_next,
            (
                objective_grad[block_start : block_start + block_len, 0],
                inflow,
                fault_current[block_start : block_start + block_len],
            ),
            reverse=True,
        )
        samples = jnp.dot(
            adjoint_block.reshape(block_len * scen_rows, node_count), pick_table, precision=PRECISE
        )
        series = (
            jnp.transpose(
                samples[:, :port_total].reshape(block_len, scen_rows, 4, slot_count), (2, 3, 0, 1)
            )
            * live_mask[:, :, None, None]
        )
        outbound = series.reshape(4, slot_count, block_len * scen_rows)
        control_term = jnp.sum(
            samples[:, port_total:].reshape(block_len, scen_rows, conv_count)
            * conv_drive[0, block_start : block_start + block_len],
            axis=(0, 1),
        )
        fault_term = jnp.sum(
            jnp.sum(adjoint_block * fault_table[None], axis=2)
            * fault_voltage[block_start : block_start + block_len],
            axis=0,
        )
        control_local = control_local + lax.psum(control_term, "scen")
        fault_local = fault_local + lax.psum(fault_term, "sub")
        received = jnp.stack(
            [
                passed_along(outbound[opposite[direction]], "sub", -offsets[direction])
                for direction in range(4)
            ]
        )
        window = jnp.concatenate(
            [received.reshape(4, slot_count, block_len, scen_rows), window[:, :, :block_len]],
            axis=2,
        )
    return (adjoint_next[None], window[None], control_local[None], fault_local)


def solution(mesh):
    return jax.shard_map(
        body,
        mesh=mesh,
        in_specs=(
            P("sub", None, None),
            P(None, "sub", "scen", None),
            P("sub", "scen", None),
            P("sub", None),
            P("sub", None, None),
            P("sub", None),
            P("sub", None, None),
            P("sub", None, None),
            P("sub", None, None, None, "scen"),
            P("sub", None),
            P("sub", None, "scen", None),
            P("scen"),
            P(None, "scen"),
            P(None, "scen"),
        ),
        out_specs=(
            P("sub", "scen", None),
            P("sub", None, None, None, "scen"),
            P("sub", None),
            P("scen"),
        ),
        check_vma=False,
    )
```

profile of v0, /device:TPU:64, one launch (start us, length us, event | category | flops | bytes accessed | tf_op | source)
XLA Modules:
  0.0 630.8 jit_solution(12138053387449394268)
XLA Ops:
  6.0 2.4 slice_bitcast_fusion
  9.2 2.0 fusion.45
  12.6 46.1 %while.34 = (s32[]{:T(128)}, f32[16,1024]{1,0:T(8,128)S(1)}, f32[24,16,1024]{2,1,0:T(8,128)}, bf16[24,16,1024]{2,1,0:T(8,128)(2,1)}, f32[1,1024]{1,0:T(1,128)S(1...) while((s32[]{:T(128)}, f32[16,1024]{1,0:T(8,128)S(1)}, ...), condition=%wide.region_1.2_spmd.clone, body=%wide.region_0.1_spmd.clone.sunk | while | flops 33685504 | bytes 2528637 | solution.py:93
  12.7 1.9 bitcast_dynamic-update-slice_fusion.4
  14.6 1.9 bitcast_dynamic-update-slice_fusion.4
  16.5 1.9 bitcast_dynamic-update-slice_fusion.4
  18.4 1.9 bitcast_dynamic-update-slice_fusion.4
  20.4 1.9 bitcast_dynamic-update-slice_fusion.4
  22.3 1.9 bitcast_dynamic-update-slice_fusion.4
  24.2 1.9 bitcast_dynamic-update-slice_fusion.4
  26.1 1.9 bitcast_dynamic-update-slice_fusion.4
  28.0 1.9 bitcast_dynamic-update-slice_fusion.4
  33.8 1.9 bitcast_dynamic-update-slice_fusion.4
  35.7 1.9 bitcast_dynamic-update-slice_fusion.4
  37.6 1.9 bitcast_dynamic-update-slice_fusion.4
  39.6 1.9 bitcast_dynamic-update-slice_fusion.4
  41.5 1.9 bitcast_dynamic-update-slice_fusion.4
  43.4 1.9 bitcast_dynamic-update-slice_fusion.4
  45.3 1.9 bitcast_dynamic-update-slice_fusion.4
  49.2 1.9 bitcast_dynamic-update-slice_fusion.4
  51.1 1.9 bitcast_dynamic-update-slice_fusion.4
  53.0 1.9 bitcast_dynamic-update-slice_fusion.4
  54.9 1.9 bitcast_dynamic-update-slice_fusion.4
  58.9 2.3 fusion.57
  63.5 14.5 %collective-permute-start = (f32[8,384]{1,0:T(8,128)}, f32[8,384]{1,0:T(8,128)S(1)}, u32[]{:S(2)}, u32[]{:S(2)}) collective-permute-start(f32[8,384]{1,0:T(8,128)} %squeeze.91), channel_id=1, source_target_pairs={{0,508},{4,0},{8,4},{12,8},{16,12},{20,16},{24,20},{28,24},{32,28}... | collective-permute-start | bytes 36872 | tf_op jit(solution)/shard_map/ppermute | solution.py:12
  78.1 1.9 collective-permute-start.1
  80.8 5.3 collective-permute-start.2
  86.2 4.4 collective-permute-start.3
  98.0 4.7 collective-permute-done.3
  105.3 2.0 fusion.43
  108.7 62.3 %while.35 = (s32[]{:T(128)}, f32[16,1024]{1,0:T(8,128)S(1)}, f32[24,16,1024]{2,1,0:T(8,128)}, bf16[24,16,1024]{2,1,0:T(8,128)(2,1)S(1)}, f32[1,1024]{1,0:T(1,128...) while((s32[]{:T(128)}, f32[16,1024]{1,0:T(8,128)S(1)}, ...), condition=%wide.region_3.4_spmd.clone, body=%wide.region_2.3_spmd.clone.sunk | while | flops 33685504 | bytes 2529533 | solution.py:93
  109.4 1.9 bitcast_dynamic-update-slice_fusion.5
  114.6 1.9 bitcast_dynamic-update-slice_fusion.5
  117.2 1.9 bitcast_dynamic-update-slice_fusion.5
  122.4 1.9 bitcast_dynamic-update-slice_fusion.5
  125.0 1.9 bitcast_dynamic-update-slice_fusion.5
  127.6 1.9 bitcast_dynamic-update-slice_fusion.5
  132.8 1.9 bitcast_dynamic-update-slice_fusion.5
  145.8 1.9 bitcast_dynamic-update-slice_fusion.5
  151.0 1.9 bitcast_dynamic-update-slice_fusion.5
  166.5 1.9 bitcast_dynamic-update-slice_fusion.5
  171.0 2.3 multiply_reduce_fusion
  174.8 13.4 %collective-permute-start.4 = (f32[8,384]{1,0:T(8,128)S(1)}, f32[8,384]{1,0:T(8,128)S(1)}, u32[]{:S(2)}, u32[]{:S(2)}) collective-permute-start(f32[8,384]{1,0:T(8,128)S(1)} %squeeze.95), channel_id=1, source_target_pairs={{0,508},{4,0},{8,4},{12,8},{16,12},{20,16},{24,20},{28,24},{32,28}... | collective-permute-start | bytes 36872 | tf_op jit(solution)/shard_map/ppermute | solution.py:12
  188.3 1.9 collective-permute-start.5
  190.3 1.9 collective-permute-start.6
  192.3 7.8 %collective-permute-start.7 = (f32[8,384]{1,0:T(8,128)S(1)}, f32[8,384]{1,0:T(8,128)S(1)}, u32[]{:S(2)}, u32[]{:S(2)}) collective-permute-start(f32[8,384]{1,0:T(8,128)S(1)} %squeeze.98), channel_id=1, source_target_pairs={{0,32},{4,36},{8,40},{12,44},{16,48},{20,52},{24,56},{28,60},{32,6... | collective-permute-start | bytes 36872 | tf_op jit(solution)/shard_map/ppermute | solution.py:12
  201.1 417.3 %psum.33 = f32[16]{0:T(128)} all-reduce(f32[16]{0:T(128)S(1)} %add.136), channel_id=1, replica_groups=mesh['sub'=128,'scen'=4] {'sub'}, use_global_device_ids=true, to_apply=%region_10.11 | all-reduce | flops 16 | bytes 128 | tf_op jit(solution)/shard_map/psum | solution.py:124
  618.5 10.8 %psum.32 = f32[16]{0:T(128)} all-reduce(f32[16]{0:T(128)S(1)} %add.135), channel_id=1, replica_groups=mesh['sub'=128,'scen'=4] {'scen'}, use_global_device_ids=true, to_apply=%region_5.6 | all-reduce | flops 16 | bytes 128 | tf_op jit(solution)/shard_map/psum | solution.py:123
  (246 shorter events, 76.9 us)
Async XLA Ops:
  3.6 5.6 copy-start.24
  6.0 2.5 copy-start.20
  8.4 2.8 copy-start.29
  9.2 49.7 %copy-start.11 = (pred[1024,32]{0,1:T(8,128)(4,1)}, pred[1024,32]{0,1:T(8,128)(4,1)S(1)}, u32[]{:S(2)}) copy-start(pred[1024,32]{0,1:T(8,128)(4,1)S(1)} %iota_compare_fusion.5) | copy-start | bytes 98308
  9.2 3.4 copy-start.26
  9.2 3.4 copy-start
  9.2 3.4 copy-start.3
  9.2 3.4 copy-start.9
  12.6 46.2 %copy-start.28 = (s32[1,16]{1,0:T(1,128)S(1)}, s32[1,16]{1,0:T(1,128)}, u32[]{:S(2)}) copy-start(s32[1,16]{1,0:T(1,128)} %param.27) | copy-start | bytes 196
  58.8 2.3 copy-start.14
  61.2 0.6 copy-start.10
  61.8 29.5 %copy-start.8 = (f32[1,48,16,16]{1,3,2,0:T(8,128)S(1)}, f32[1,48,16,16]{1,3,2,0:T(8,128)}, u32[]{:S(2)}) copy-start(f32[1,48,16,16]{1,3,2,0:T(8,128)} %param.28) | copy-start | bytes 147460
  61.8 30.2 %copy-start.21 = (f32[48,16]{0,1:T(8,128)S(1)}, f32[48,16]{0,1:T(8,128)}, u32[]{:S(2)}) copy-start(f32[48,16]{0,1:T(8,128)} %param.31) | copy-start | bytes 9220
  62.0 30.1 %copy-start.22 = (f32[24,16]{0,1:T(8,128)S(1)}, f32[24,16]{0,1:T(8,128)}, u32[]{:S(2)}) copy-start(f32[24,16]{0,1:T(8,128)} %get-tuple-element.466) | copy-start | bytes 4612
  63.5 33.2 %collective-permute-start = (f32[8,384]{1,0:T(8,128)}, f32[8,384]{1,0:T(8,128)S(1)}, u32[]{:S(2)}, u32[]{:S(2)}) collective-permute-start(f32[8,384]{1,0:T(8,128)} %squeeze.91), channel_id=1, source_target_pairs={{0,508},{4,0},{8,4},{12,8},{16,12},{20,16},{24,20},{28,24},{32,28}... | collective-permute-start | bytes 36872 | tf_op jit(solution)/shard_map/ppermute | solution.py:12
  78.1 18.7 %collective-permute-start.1 = (f32[8,384]{1,0:T(8,128)S(1)}, f32[8,384]{1,0:T(8,128)S(1)}, u32[]{:S(2)}, u32[]{:S(2)}) collective-permute-start(f32[8,384]{1,0:T(8,128)S(1)} %squeeze.92), channel_id=1, source_target_pairs={{0,4},{4,8},{8,12},{12,16},{16,20},{20,24},{24,28},{28,32},{32,36}... | collective-permute-start | bytes 36872 | tf_op jit(solution)/shard_map/ppermute | solution.py:12
  80.8 16.3 %collective-permute-start.2 = (f32[8,384]{1,0:T(8,128)}, f32[8,384]{1,0:T(8,128)}, u32[]{:S(2)}, u32[]{:S(2)}) collective-permute-start(f32[8,384]{1,0:T(8,128)} %squeeze.93), channel_id=1, source_target_pairs={{0,480},{4,484},{8,488},{12,492},{16,496},{20,500},{24,504},{28,50... | collective-permute-start | bytes 36872 | tf_op jit(solution)/shard_map/ppermute | solution.py:12
  86.2 16.5 %collective-permute-start.3 = (f32[8,384]{1,0:T(8,128)S(1)}, f32[8,384]{1,0:T(8,128)}, u32[]{:S(2)}, u32[]{:S(2)}) collective-permute-start(f32[8,384]{1,0:T(8,128)S(1)} %squeeze.94), channel_id=1, source_target_pairs={{0,32},{4,36},{8,40},{12,44},{16,48},{20,52},{24,56},{28,60},{32,6... | collective-permute-start | bytes 36872 | tf_op jit(solution)/shard_map/ppermute | solution.py:12
  95.1 10.2 %copy-start.25 = (s32[32]{0:T(128)S(1)}, s32[32]{0:T(128)}, u32[]{:S(2)}) copy-start(s32[32]{0:T(128)} %copy-done.24) | copy-start | bytes 388
  95.1 10.2 %copy-start.27 = (f32[32]{0:T(128)S(1)}, f32[32]{0:T(128)}, u32[]{:S(2)}) copy-start(f32[32]{0:T(128)} %copy-done.26) | copy-start | bytes 388
  97.9 7.2 %copy-start.4 = (f32[1,8,24,16]{2,3,1,0:T(8,128)}, f32[1,8,24,16]{2,3,1,0:T(8,128)S(1)}, u32[]{:S(2)}) copy-start(f32[1,8,24,16]{2,3,1,0:T(8,128)S(1)} %copy.48) | copy-start | bytes 36868
  103.6 1.6 copy-start.6
  108.7 62.3 %copy-start.13 = (f32[16,1024]{1,0:T(8,128)S(1)}, f32[16,1024]{1,0:T(8,128)}, u32[]{:S(2)}) copy-start(f32[16,1024]{1,0:T(8,128)} %fusion.55) | copy-start | bytes 196612
  171.0 2.3 copy-start.2
  171.0 2.4 copy-start.1
  171.0 2.4 copy-start.12
  171.0 2.4 copy-start.15
  173.3 1.2 copy-start.23
  174.3 25.9 %copy-start.16 = (f32[384,16]{0,1:T(8,128)S(1)}, f32[384,16]{0,1:T(8,128)}, u32[]{:S(2)}) copy-start(f32[384,16]{0,1:T(8,128)} %squeeze.100) | copy-start | bytes 73732
  174.3 25.9 %copy-start.17 = (f32[384,16]{0,1:T(8,128)S(1)}, f32[384,16]{0,1:T(8,128)}, u32[]{:S(2)}) copy-start(f32[384,16]{0,1:T(8,128)} %squeeze.99) | copy-start | bytes 73732
  174.3 26.8 %copy-start.18 = (f32[24,16]{1,0:T(8,128)S(1)}, f32[24,16]{1,0:T(8,128)}, u32[]{:S(2)}) copy-start(f32[24,16]{1,0:T(8,128)} %copy.62) | copy-start | bytes 4612
  174.3 26.8 %copy-start.19 = (f32[24,16]{1,0:T(8,128)S(1)}, f32[24,16]{1,0:T(8,128)}, u32[]{:S(2)}) copy-start(f32[24,16]{1,0:T(8,128)} %copy.63) | copy-start | bytes 4612
  174.5 455.5 %copy-start.5 = (f32[1,8,24,16]{2,3,1,0:T(8,128)S(1)}, f32[1,8,24,16]{2,3,1,0:T(8,128)}, u32[]{:S(2)}) copy-start(f32[1,8,24,16]{2,3,1,0:T(8,128)} %copy-done.4) | copy-start | bytes 36868
  174.5 455.5 %copy-start.7 = (f32[1,8,24,16]{2,3,1,0:T(8,128)S(1)}, f32[1,8,24,16]{2,3,1,0:T(8,128)}, u32[]{:S(2)}) copy-start(f32[1,8,24,16]{2,3,1,0:T(8,128)} %copy-done.6) | copy-start | bytes 36868
  174.8 454.5 %collective-permute-start.4 = (f32[8,384]{1,0:T(8,128)S(1)}, f32[8,384]{1,0:T(8,128)S(1)}, u32[]{:S(2)}, u32[]{:S(2)}) collective-permute-start(f32[8,384]{1,0:T(8,128)S(1)} %squeeze.95), channel_id=1, source_target_pairs={{0,508},{4,0},{8,4},{12,8},{16,12},{20,16},{24,20},{28,24},{32,28}... | collective-permute-start | bytes 36872 | tf_op jit(solution)/shard_map/ppermute | solution.py:12
  188.3 441.1 %collective-permute-start.5 = (f32[8,384]{1,0:T(8,128)S(1)}, f32[8,384]{1,0:T(8,128)S(1)}, u32[]{:S(2)}, u32[]{:S(2)}) collective-permute-start(f32[8,384]{1,0:T(8,128)S(1)} %squeeze.96), channel_id=1, source_target_pairs={{0,4},{4,8},{8,12},{12,16},{16,20},{20,24},{24,28},{28,32},{32,36}... | collective-permute-start | bytes 36872 | tf_op jit(solution)/shard_map/ppermute | solution.py:12
  190.3 439.3 %collective-permute-start.6 = (f32[8,384]{1,0:T(8,128)S(1)}, f32[8,384]{1,0:T(8,128)S(1)}, u32[]{:S(2)}, u32[]{:S(2)}) collective-permute-start(f32[8,384]{1,0:T(8,128)S(1)} %squeeze.97), channel_id=1, source_target_pairs={{0,480},{4,484},{8,488},{12,492},{16,496},{20,500},{24,504},{28,50... | collective-permute-start | bytes 36872 | tf_op jit(solution)/shard_map/ppermute | solution.py:12
  192.3 437.4 %collective-permute-start.7 = (f32[8,384]{1,0:T(8,128)S(1)}, f32[8,384]{1,0:T(8,128)S(1)}, u32[]{:S(2)}, u32[]{:S(2)}) collective-permute-start(f32[8,384]{1,0:T(8,128)S(1)} %squeeze.98), channel_id=1, source_target_pairs={{0,32},{4,36},{8,40},{12,44},{16,48},{20,52},{24,56},{28,60},{32,6... | collective-permute-start | bytes 36872 | tf_op jit(solution)/shard_map/ppermute | solution.py:12
where the time goes:
time: 635 us; the launch traced here: 631 us
  blocking collectives  428 us (67%)
  matrix products  102 us (16%)
  starting transfers between devices  51.3 us (8%)
  local copies, waits for them, and re-layouts  35.8 us (6%)
  other arithmetic  7.83 us (1%)
    psum x1, blocking collectives, body(): fault_local = fault_local + lax.psum(fault_term, 'sub')  417 us
    dot_general x48, matrix products, one_step(): jnp.dot(right_side.astype(jnp.bfloat16), weights, preferred_element_type=...  91.4 us
    ppermute x8, starting transfers between devices, passed_along(): return lax.ppermute(value, axis, pairs)  51.3 us
    mul x48, local copies, waits for them, and re-layouts, one_step(): current_now[:, None] * fault_table  16.6 us
  transfers between devices with their start and end apart: 8, of which 1 were waited for; matrix products, arithmetic and copies ran while one was open for 2% of the time, Pallas kernels for 0%

commit v1 on v0

--- a/solution.py
+++ b/solution.py
@@ -121,7 +121,11 @@
             axis=0,
         )
         control_local = control_local + lax.psum(control_term, "scen")
-        fault_local = fault_local + lax.psum(fault_term, "sub")
+
+        def _launch_keys(piece_in, row_axis):
+            return jax.lax.all_gather(piece_in, row_axis).sum(axis=0)
+
+        fault_local = fault_local + _launch_keys(fault_term, "sub")
         received = jnp.stack(
             [
                 passed_along(outbound[opposite[direction]], "sub", -offsets[direction])

time: 635 us -> 1040 us (1.64)
  blocking collectives: 428 us -> 827 us
    unnamed x0 -> x1, blocking collectives: none -> 815 us
    psum x1 -> x0, blocking collectives: 417 us -> none  [body(): fault_local = fault_local + lax.psum(fault_term, 'sub')]
  transfers between devices with their start and end apart: 8 -> 8, of which waited for: 1 -> 1; matrix products, arithmetic and copies ran while one was open for 2% -> 1% of each run, Pallas kernels for 0% -> 0%
where the time goes in v1:
time: 1040 us; the launch traced here: 1030 us
  blocking collectives  827 us (80%)
  matrix products  101 us (10%)
  starting transfers between devices  53.2 us (5%)
  local copies, waits for them, and re-layouts  37.7 us (4%)
    unnamed x1, blocking collectives  815 us
    dot_general x48, matrix products, one_step(): jnp.dot(right_side.astype(jnp.bfloat16), weights, preferred_element_type=...  91 us
    ppermute x8, starting transfers between devices, passed_along(): return lax.ppermute(value, axis, pairs)  53.2 us
  transfers between devices with their start and end apart: 8, of which 1 were waited for; matrix products, arithmetic and copies ran while one was open for 1% of the time, Pallas kernels for 0%

profile of v1, /device:TPU:64, one launch (start us, length us, event | category | flops | bytes accessed | tf_op | source)
XLA Modules:
  0.0 1032.2 jit_solution(126828645566387175)
XLA Ops:
  5.9 2.4 slice_bitcast_fusion
  9.2 2.0 fusion.45
  12.6 45.9 %while.34 = (s32[]{:T(128)}, f32[16,1024]{1,0:T(8,128)S(1)}, f32[24,16,1024]{2,1,0:T(8,128)}, bf16[24,16,1024]{2,1,0:T(8,128)(2,1)}, f32[1,1024]{1,0:T(1,128)S(1...) while((s32[]{:T(128)}, f32[16,1024]{1,0:T(8,128)S(1)}, ...), condition=%wide.region_1.2_spmd.clone, body=%wide.region_0.1_spmd.clone.sunk | while | flops 33685504 | bytes 2528637 | solution.py:93
  12.6 1.9 bitcast_dynamic-update-slice_fusion.4
  14.5 1.9 bitcast_dynamic-update-slice_fusion.4
  16.4 1.9 bitcast_dynamic-update-slice_fusion.4
  18.3 1.9 bitcast_dynamic-update-slice_fusion.4
  20.3 1.9 bitcast_dynamic-update-slice_fusion.4
  22.2 1.9 bitcast_dynamic-update-slice_fusion.4
  24.1 1.9 bitcast_dynamic-update-slice_fusion.4
  26.0 1.9 bitcast_dynamic-update-slice_fusion.4
  27.9 1.9 bitcast_dynamic-update-slice_fusion.4
  31.7 1.9 bitcast_dynamic-update-slice_fusion.4
  35.6 1.9 bitcast_dynamic-update-slice_fusion.4
  39.4 1.9 bitcast_dynamic-update-slice_fusion.4
  41.3 1.9 bitcast_dynamic-update-slice_fusion.4
  43.2 1.9 bitcast_dynamic-update-slice_fusion.4
  45.1 1.9 bitcast_dynamic-update-slice_fusion.4
  47.0 1.9 bitcast_dynamic-update-slice_fusion.4
  48.9 1.9 bitcast_dynamic-update-slice_fusion.4
  52.8 1.9 bitcast_dynamic-update-slice_fusion.4
  54.7 1.9 bitcast_dynamic-update-slice_fusion.4
  56.6 1.9 bitcast_dynamic-update-slice_fusion.4
  58.6 2.3 fusion.57
  63.2 14.5 %collective-permute-start = (f32[8,384]{1,0:T(8,128)}, f32[8,384]{1,0:T(8,128)S(1)}, u32[]{:S(2)}, u32[]{:S(2)}) collective-permute-start(f32[8,384]{1,0:T(8,128)} %squeeze.91), channel_id=1, source_target_pairs={{0,508},{4,0},{8,4},{12,8},{16,12},{20,16},{24,20},{28,24},{32,28}... | collective-permute-start | bytes 36872 | tf_op jit(solution)/shard_map/ppermute | solution.py:12
  77.9 1.9 collective-permute-start.1
  80.5 5.3 collective-permute-start.2
  85.9 4.4 collective-permute-start.3
  99.6 2.8 collective-permute-done.3
  105.1 2.0 fusion.43
  108.4 62.1 %while.35 = (s32[]{:T(128)}, f32[16,1024]{1,0:T(8,128)S(1)}, f32[24,16,1024]{2,1,0:T(8,128)}, bf16[24,16,1024]{2,1,0:T(8,128)(2,1)S(1)}, f32[1,1024]{1,0:T(1,128...) while((s32[]{:T(128)}, f32[16,1024]{1,0:T(8,128)S(1)}, ...), condition=%wide.region_3.4_spmd.clone, body=%wide.region_2.3_spmd.clone.sunk | while | flops 33685504 | bytes 2529533 | solution.py:93
  114.3 1.9 bitcast_dynamic-update-slice_fusion.5
  119.5 1.9 bitcast_dynamic-update-slice_fusion.5
  124.7 1.9 bitcast_dynamic-update-slice_fusion.5
  127.2 1.9 bitcast_dynamic-update-slice_fusion.5
  129.8 1.9 bitcast_dynamic-update-slice_fusion.5
  135.0 1.9 bitcast_dynamic-update-slice_fusion.5
  142.7 1.9 bitcast_dynamic-update-slice_fusion.5
  147.9 1.9 bitcast_dynamic-update-slice_fusion.5
  155.7 1.9 bitcast_dynamic-update-slice_fusion.5
  158.2 1.9 bitcast_dynamic-update-slice_fusion.5
  170.5 2.3 multiply_reduce_fusion
  174.3 15.4 %collective-permute-start.4 = (f32[8,384]{1,0:T(8,128)S(1)}, f32[8,384]{1,0:T(8,128)S(1)}, u32[]{:S(2)}, u32[]{:S(2)}) collective-permute-start(f32[8,384]{1,0:T(8,128)S(1)} %squeeze.95), channel_id=1, source_target_pairs={{0,508},{4,0},{8,4},{12,8},{16,12},{20,16},{24,20},{28,24},{32,28}... | collective-permute-start | bytes 36872 | tf_op jit(solution)/shard_map/ppermute | solution.py:12
  189.7 1.9 collective-permute-start.5
  191.8 1.9 collective-permute-start.6
  193.8 7.8 collective-permute-start.7
  203.1 814.6 %all-reduce.2 = (f32[2048]{0:T(1024)S(1)}, f32[2048]{0:T(1024)S(1)}) all-reduce(f32[2048]{0:T(1024)S(1)} %dynamic-update-slice, f32[2048]{0:T(1024)S(1)} %dynamic-update-slice.1), channel_id=2, replica_groups=mesh['sub'=128,'scen'=4] {'sub'}, use_global_device_ids=true, to_apply=%add | all-reduce | flops 4096 | bytes 32768
  1018.4 12.2 %psum.16 = f32[16]{0:T(128)} all-reduce(f32[16]{0:T(128)S(1)} %add.131), channel_id=1, replica_groups=mesh['sub'=128,'scen'=4] {'scen'}, use_global_device_ids=true, to_apply=%region_5.6 | all-reduce | flops 16 | bytes 128 | tf_op jit(solution)/shard_map/psum | solution.py:123
  (255 shorter events, 79.3 us)
Async XLA Ops:
  3.5 5.6 copy-start.24
  5.9 2.4 copy-start.20
  8.4 2.8 copy-start.29
  9.1 49.5 %copy-start.11 = (pred[1024,32]{0,1:T(8,128)(4,1)}, pred[1024,32]{0,1:T(8,128)(4,1)S(1)}, u32[]{:S(2)}) copy-start(pred[1024,32]{0,1:T(8,128)(4,1)S(1)} %iota_compare_fusion.5) | copy-start | bytes 98308
  9.2 3.4 copy-start.26
  9.2 3.4 copy-start
  9.2 3.4 copy-start.3
  9.2 3.3 copy-start.9
  12.5 45.9 %copy-start.28 = (s32[1,16]{1,0:T(1,128)S(1)}, s32[1,16]{1,0:T(1,128)}, u32[]{:S(2)}) copy-start(s32[1,16]{1,0:T(1,128)} %param.27) | copy-start | bytes 196
  58.6 2.3 copy-start.14
  60.9 0.6 copy-start.10
  61.5 29.5 %copy-start.8 = (f32[1,48,16,16]{1,3,2,0:T(8,128)S(1)}, f32[1,48,16,16]{1,3,2,0:T(8,128)}, u32[]{:S(2)}) copy-start(f32[1,48,16,16]{1,3,2,0:T(8,128)} %param.28) | copy-start | bytes 147460
  61.5 30.2 %copy-start.21 = (f32[48,16]{0,1:T(8,128)S(1)}, f32[48,16]{0,1:T(8,128)}, u32[]{:S(2)}) copy-start(f32[48,16]{0,1:T(8,128)} %param.31) | copy-start | bytes 9220
  61.7 30.1 %copy-start.22 = (f32[24,16]{0,1:T(8,128)S(1)}, f32[24,16]{0,1:T(8,128)}, u32[]{:S(2)}) copy-start(f32[24,16]{0,1:T(8,128)} %get-tuple-element.468) | copy-start | bytes 4612
  63.2 35.1 %collective-permute-start = (f32[8,384]{1,0:T(8,128)}, f32[8,384]{1,0:T(8,128)S(1)}, u32[]{:S(2)}, u32[]{:S(2)}) collective-permute-start(f32[8,384]{1,0:T(8,128)} %squeeze.91), channel_id=1, source_target_pairs={{0,508},{4,0},{8,4},{12,8},{16,12},{20,16},{24,20},{28,24},{32,28}... | collective-permute-start | bytes 36872 | tf_op jit(solution)/shard_map/ppermute | solution.py:12
  77.9 20.7 %collective-permute-start.1 = (f32[8,384]{1,0:T(8,128)S(1)}, f32[8,384]{1,0:T(8,128)S(1)}, u32[]{:S(2)}, u32[]{:S(2)}) collective-permute-start(f32[8,384]{1,0:T(8,128)S(1)} %squeeze.92), channel_id=1, source_target_pairs={{0,4},{4,8},{8,12},{12,16},{16,20},{20,24},{24,28},{28,32},{32,36}... | collective-permute-start | bytes 36872 | tf_op jit(solution)/shard_map/ppermute | solution.py:12
  80.5 18.2 %collective-permute-start.2 = (f32[8,384]{1,0:T(8,128)}, f32[8,384]{1,0:T(8,128)}, u32[]{:S(2)}, u32[]{:S(2)}) collective-permute-start(f32[8,384]{1,0:T(8,128)} %squeeze.93), channel_id=1, source_target_pairs={{0,480},{4,484},{8,488},{12,492},{16,496},{20,500},{24,504},{28,50... | collective-permute-start | bytes 36872 | tf_op jit(solution)/shard_map/ppermute | solution.py:12
  85.9 16.5 %collective-permute-start.3 = (f32[8,384]{1,0:T(8,128)S(1)}, f32[8,384]{1,0:T(8,128)}, u32[]{:S(2)}, u32[]{:S(2)}) collective-permute-start(f32[8,384]{1,0:T(8,128)S(1)} %squeeze.94), channel_id=1, source_target_pairs={{0,32},{4,36},{8,40},{12,44},{16,48},{20,52},{24,56},{28,60},{32,6... | collective-permute-start | bytes 36872 | tf_op jit(solution)/shard_map/ppermute | solution.py:12
  94.8 10.2 copy-start.25
  94.9 10.2 copy-start.27
  99.6 5.2 copy-start.4
  103.3 1.6 copy-start.6
  108.4 62.1 %copy-start.13 = (f32[16,1024]{1,0:T(8,128)S(1)}, f32[16,1024]{1,0:T(8,128)}, u32[]{:S(2)}) copy-start(f32[16,1024]{1,0:T(8,128)} %fusion.55) | copy-start | bytes 196612
  170.5 2.3 copy-start.2
  170.5 2.4 copy-start.1
  170.5 2.4 copy-start.12
  170.5 2.4 copy-start.15
  172.8 1.2 copy-start.23
  173.8 27.9 %copy-start.16 = (f32[384,16]{0,1:T(8,128)S(1)}, f32[384,16]{0,1:T(8,128)}, u32[]{:S(2)}) copy-start(f32[384,16]{0,1:T(8,128)} %squeeze.100) | copy-start | bytes 73732
  173.8 27.9 %copy-start.17 = (f32[384,16]{0,1:T(8,128)S(1)}, f32[384,16]{0,1:T(8,128)}, u32[]{:S(2)}) copy-start(f32[384,16]{0,1:T(8,128)} %squeeze.99) | copy-start | bytes 73732
  173.8 28.7 %copy-start.18 = (f32[24,16]{1,0:T(8,128)S(1)}, f32[24,16]{1,0:T(8,128)}, u32[]{:S(2)}) copy-start(f32[24,16]{1,0:T(8,128)} %copy.62) | copy-start | bytes 4612
  173.8 28.7 %copy-start.19 = (f32[24,16]{1,0:T(8,128)S(1)}, f32[24,16]{1,0:T(8,128)}, u32[]{:S(2)}) copy-start(f32[24,16]{1,0:T(8,128)} %copy.63) | copy-start | bytes 4612
  174.1 857.2 %copy-start.5 = (f32[1,8,24,16]{2,3,1,0:T(8,128)S(1)}, f32[1,8,24,16]{2,3,1,0:T(8,128)}, u32[]{:S(2)}) copy-start(f32[1,8,24,16]{2,3,1,0:T(8,128)} %copy-done.4) | copy-start | bytes 36868
  174.1 857.2 %copy-start.7 = (f32[1,8,24,16]{2,3,1,0:T(8,128)S(1)}, f32[1,8,24,16]{2,3,1,0:T(8,128)}, u32[]{:S(2)}) copy-start(f32[1,8,24,16]{2,3,1,0:T(8,128)} %copy-done.6) | copy-start | bytes 36868
  174.3 856.3 %collective-permute-start.4 = (f32[8,384]{1,0:T(8,128)S(1)}, f32[8,384]{1,0:T(8,128)S(1)}, u32[]{:S(2)}, u32[]{:S(2)}) collective-permute-start(f32[8,384]{1,0:T(8,128)S(1)} %squeeze.95), channel_id=1, source_target_pairs={{0,508},{4,0},{8,4},{12,8},{16,12},{20,16},{24,20},{28,24},{32,28}... | collective-permute-start | bytes 36872 | tf_op jit(solution)/shard_map/ppermute | solution.py:12
  189.7 841.0 %collective-permute-start.5 = (f32[8,384]{1,0:T(8,128)S(1)}, f32[8,384]{1,0:T(8,128)S(1)}, u32[]{:S(2)}, u32[]{:S(2)}) collective-permute-start(f32[8,384]{1,0:T(8,128)S(1)} %squeeze.96), channel_id=1, source_target_pairs={{0,4},{4,8},{8,12},{12,16},{16,20},{20,24},{24,28},{28,32},{32,36}... | collective-permute-start | bytes 36872 | tf_op jit(solution)/shard_map/ppermute | solution.py:12
  191.8 839.2 %collective-permute-start.6 = (f32[8,384]{1,0:T(8,128)S(1)}, f32[8,384]{1,0:T(8,128)S(1)}, u32[]{:S(2)}, u32[]{:S(2)}) collective-permute-start(f32[8,384]{1,0:T(8,128)S(1)} %squeeze.97), channel_id=1, source_target_pairs={{0,480},{4,484},{8,488},{12,492},{16,496},{20,500},{24,504},{28,50... | collective-permute-start | bytes 36872 | tf_op jit(solution)/shard_map/ppermute | solution.py:12
  193.8 837.4 %collective-permute-start.7 = (f32[8,384]{1,0:T(8,128)S(1)}, f32[8,384]{1,0:T(8,128)S(1)}, u32[]{:S(2)}, u32[]{:S(2)}) collective-permute-start(f32[8,384]{1,0:T(8,128)S(1)} %squeeze.98), channel_id=1, source_target_pairs={{0,32},{4,36},{8,40},{12,44},{16,48},{20,52},{24,56},{28,60},{32,6... | collective-permute-start | bytes 36872 | tf_op jit(solution)/shard_map/ppermute | solution.py:12
